TPU v7x, 512 devices: a whole 4x8x8 slice. The times are simulated.
512 devices in a mesh: seq: 64 (over y, z_lo, x), ch: 8 (over z_hi, core).
Axes of the slice: x: 4, y: 8, z: 8 (z_hi: 4, z_lo: 2; z = z_hi * 2 + z_lo), core: 2. Of those that a mesh axis runs over, the one named last changes fastest.
Arguments:
- inputs: bfloat16 [16384, 1024], P('seq', 'ch'), may hold values from -6 to 6
- gate_values: bfloat16 [16384, 1024], P('seq', 'ch'), may hold values from -600 to 1100
- causal_filter: bfloat16 [16384, 1024], P('seq', 'ch'), may hold values from -0.046875 to 0.046875
- anti_filter: bfloat16 [16384, 1024], P('seq', 'ch'), may hold values from -0.046875 to 0.046875
- skip_gain: float32 [1024], P('ch'), may hold values from 0.25 to 1.75
- norm_gain: float32 [1024], P('ch'), may hold values from 0.25 to 1.75
Outputs:
- mixer_out: bfloat16 [16384, 1024], P('seq', 'ch')
All inputs are finite; a program needn't handle non-finite values.
Results may differ from a plain program's by a relative error of at most 0.007.
Values may be sent and summed in bfloat16 or wider, within the bound.
No kernel may reach another device: no remote copies, remote signals or barrier semaphores. Data moves between devices by JAX's collectives and lax.ppermute only.
A program may use at most 128 MiB of HBM per device.

v0:
```python
import numpy as np
import jax
import jax.numpy as jnp
from jax import lax
from jax.sharding import PartitionSpec as P

D = 1024
HIGHEST = lax.Precision.HIGHEST


def padded(count, unit=8):
    return -(-count // unit) * unit


def inner_tables(rows_dev):
    freqs = rows_dev + 1
    fp = padded(freqs)
    f = np.arange(freqs)[:, None]
    n = np.arange(rows_dev)[None, :]
    phase = f * n % (2 * rows_dev) * (np.pi / rows_dev)
    fwd = np.zeros((2 * fp, rows_dev))
    fwd[:freqs] = np.cos(phase)
    fwd[fp : fp + freqs] = -np.sin(phase)
    t = np.arange(rows_dev)[:, None] + rows_dev
    f2 = np.arange(freqs)[None, :]
    phase2 = f2 * t % (2 * rows_dev) * (np.pi / rows_dev)
    weight = np.where((f2 == 0) | (f2 == rows_dev), 1.0, 2.0) / (2 * rows_dev)
    inv = np.zeros((rows_dev, 2 * fp))
    inv[:, :freqs] = weight * np.cos(phase2)
    inv[:, fp : fp + freqs] = -weight * np.sin(phase2)
    return (fp, fwd, inv)


def outer_tables(blocks, fp):
    size = 2 * blocks
    j = np.arange(blocks)[:, None]
    m = np.arange(size)[None, :]
    phase = 2 * np.pi * (j * m % size) / size
    fwd = np.concatenate([np.cos(phase), np.sin(phase)], axis=1)
    mi = np.arange(size)[:, None]
    i = np.arange(blocks)[None, :]
    phase_i = 2 * np.pi * (mi * i % size) / size
    cos_i = np.cos(phase_i) / size
    sin_i = np.sin(phase_i) / size
    inv_re = np.concatenate([cos_i, -sin_i], axis=0)
    inv_im = np.concatenate([sin_i, cos_i], axis=0)
    sign = np.where(np.arange(fp) % 2 == 0, 1.0, -1.0)[:, None]
    step = 2 * np.pi * np.arange(size)[None, :] / size
    shift_re = np.cos(step) + sign
    shift_im = -np.sin(step) + 0.0 * sign
    return (fwd, inv_re, inv_im, shift_re, shift_im)


def on_device(inputs, gate_values, causal_filter, anti_filter, skip_gain, norm_gain):
    rows_dev, chan_dev = inputs.shape
    blocks = lax.axis_size("seq")
    per = chan_dev // blocks
    size = 2 * blocks
    f32 = jnp.float32
    own_index = lax.axis_index("seq")
    row_ids = lax.broadcasted_iota(jnp.int32, (rows_dev, 1), 0) + own_index * rows_dev
    anti_masked = jnp.where(row_ids > 0, anti_filter, jnp.zeros_like(anti_filter))
    fp, fwd_np, inv_np = inner_tables(rows_dev)
    ofwd_np, oinv_re_np, oinv_im_np, sh_re_np, sh_im_np = outer_tables(blocks, fp)
    fwd = jnp.asarray(fwd_np, jnp.bfloat16)
    inv = jnp.asarray(inv_np, f32)
    ofwd = jnp.asarray(ofwd_np, f32)
    oinv_re = jnp.asarray(oinv_re_np, f32)
    oinv_im = jnp.asarray(oinv_im_np, f32)
    sh_re = jnp.asarray(sh_re_np, f32)
    sh_im = jnp.asarray(sh_im_np, f32)
    stacked = jnp.stack([inputs, causal_filter, anti_masked])
    send = (
        stacked.reshape(3, rows_dev, blocks, per)
        .transpose(2, 0, 3, 1)
        .reshape(blocks, 3 * per * rows_dev)
    )
    recv = lax.all_to_all(send, "seq", 0, 0, tiled=True)
    series = recv.reshape(blocks, 3 * per, rows_dev).transpose(1, 0, 2)
    spec = jnp.einsum("fn,qbn->qfb", fwd, series, preferred_element_type=f32)
    spec = spec.astype(jnp.bfloat16).astype(f32)
    z = jnp.einsum("qfb,bk->qfk", spec, ofwd, precision=HIGHEST, preferred_element_type=f32)
    z_re, z_im = (z[:, :fp], z[:, fp:])
    x_re = (z_re[..., :size] + z_im[..., size:]).reshape(3, per, fp, size)
    x_im = (z_im[..., :size] - z_re[..., size:]).reshape(3, per, fp, size)
    c_re = sh_re * x_re[1] - sh_im * x_im[1]
    c_im = sh_re * x_im[1] + sh_im * x_re[1]
    a_re = sh_re * x_re[2] - sh_im * x_im[2]
    a_im = sh_re * x_im[2] + sh_im * x_re[2]
    k_re = c_re + a_re
    k_im = c_im - a_im
    y_re = k_re * x_re[0] - k_im * x_im[0]
    y_im = k_re * x_im[0] + k_im * x_re[0]
    y_cat = jnp.concatenate([y_re, y_im], axis=-1)
    t_re = jnp.einsum("cfk,ki->cfi", y_cat, oinv_re, precision=HIGHEST, preferred_element_type=f32)
    t_im = jnp.einsum("cfk,ki->cfi", y_cat, oinv_im, precision=HIGHEST, preferred_element_type=f32)
    total = jnp.concatenate([t_re, t_im], axis=1)
    conv_t = jnp.einsum("cfi,tf->cit", total, inv, precision=HIGHEST, preferred_element_type=f32)
    back = conv_t.transpose(1, 0, 2).reshape(blocks, per * rows_dev)
    got = lax.all_to_all(back, "seq", 0, 0, tiled=True)
    convolved = got.reshape(blocks * per, rows_dev).T
    gated_mix = gate_values.astype(f32) * (convolved + skip_gain[None, :] * inputs.astype(f32))
    squares = lax.psum(jnp.sum(gated_mix * gated_mix, axis=1), "ch")
    inv_norm = lax.rsqrt(squares / D + 1e-06)
    return (norm_gain[None, :] * gated_mix * inv_norm[:, None]).astype(jnp.bfloat16)


def solution(mesh):
    placed = (P("seq", "ch"), P("seq", "ch"), P("seq", "ch"), P("seq", "ch"), P("ch"), P("ch"))
    return jax.shard_map(
        on_device, mesh=mesh, in_specs=placed, out_specs=P("seq", "ch"), check_vma=False
    )
```

profile of v0, /device:TPU:1, one launch (start us, length us, event | category | flops | bytes accessed | tf_op | source)
XLA Modules:
  0.0 74.0 jit_solution(5732633215002907503)
XLA Ops:
  0.0 0.0 copy-start.1
  0.0 0.0 copy-start.7
  0.0 1.0 %copy.23 = bf16[256,128]{0,1:T(8,128)(2,1)S(1)} copy(bf16[256,128]{1,0:T(8,128)(2,1)} %param.13) | data formatting | bytes 131072 | tf_op args[0]
  1.1 0.9 %broadcast_select_fusion = bf16[256,128]{1,0:T(8,128)(2,1)S(1)} fusion(bf16[256,128]{1,0:T(8,128)(2,1)} %param.16, pred[256]{0:T(512)(128)(4,1)S(1)} %add_compare_fusion), kind=kLoop, calls=%fused_computation.22 | loop fusion | flops 32768 | bytes 131328 | tf_op jit(solution)/shard_map/jit(_where)/select_n | solution.py:62
  2.0 0.1 copy.25
  2.2 0.9 %copy.24 = bf16[256,128]{0,1:T(8,128)(2,1)S(1)} copy(bf16[256,128]{1,0:T(8,128)(2,1)} %param.15) | data formatting | bytes 131072 | tf_op args[2]
  3.1 0.3 maximum_bitcast_fusion
  3.5 0.1 copy.26
  3.6 0.1 all_to_all.16
  3.8 0.5 broadcast.18
  4.3 1.8 %reduce.2 = bf16[64,1536]{1,0:T(8,128)(2,1)S(1)} reduce(bf16[64,1,1536]{2,1,0:T(2,128)(2,1)S(1)} %all_to_all.16, bf16[]{:T(256)} %broadcast.18), dimensions={1}, to_apply=%all_to_all.16.reduce_sub_computation | reduce | bytes 393218 | tf_op jit(solution)/shard_map/all_to_all | solution.py:78
  6.1 0.1 reshape.58
  6.1 22.8 %all_to_all.20 = bf16[64,2,768]{2,1,0:T(2,128)(2,1)S(1)} all-to-all(bf16[64,2,768]{2,1,0:T(2,128)(2,1)S(1)} %reshape.58), channel_id=1, replica_groups=mesh['seq'=64,'ch'=8] {'seq'}, dimensions={0} | all-to-all | bytes 393216 | tf_op jit(solution)/shard_map/all_to_all | solution.py:78
  28.9 0.1 reshape.59
  29.0 1.1 %reduce = bf16[64,1536]{1,0:T(8,128)(2,1)S(1)} reduce(bf16[64,1,1536]{2,1,0:T(2,128)(2,1)S(1)} %reshape.59, bf16[]{:T(256)} %constant.45), dimensions={1}, to_apply=%all_to_all.13.reduce_sub_computation | reduce | bytes 393218 | tf_op jit(solution)/shard_map/all_to_all | solution.py:78
  30.2 0.0 copy-done.1
  30.2 0.3 fusion
  30.6 0.0 copy-done.7
  30.6 1.5 %fusion.11 = f32[6,528,256]{2,1,0:T(8,128)S(1)} fusion(bf16[6,528,64]{1,2,0:T(8,128)(2,1)S(1)} %fusion, f32[64,256,1]{1,0,2:T(8,128)S(1)} %copy-done.7), kind=kOutput, calls=%fused_computation.28 | convolution fusion | flops 622854144 | bytes 3715072 | tf_op jit(solution)/shard_map/qfb,bk->qfk/dot_general | solution.py:82
  32.1 0.0 copy-start.2
  32.1 0.0 copy-start.3
  32.1 0.2 slice_add_fusion
  32.3 0.0 copy-start.5
  32.3 0.0 copy-start.4
  32.3 0.0 copy-start
  32.3 0.7 copy-done.2
  33.0 0.1 copy-done.3
  33.0 0.0 copy-start.6
  33.0 0.2 multiply_subtract_fusion
  33.2 0.0 copy-start.8
  33.2 0.0 copy-start.9
  33.3 0.1 multiply_add_fusion
  33.3 0.0 copy-done.5
  33.3 0.7 fusion.2
  34.1 0.0 copy-done.4
  34.1 0.7 fusion.1
  34.8 0.0 copy-done
  34.8 0.5 convolution_bitcast_fusion
  35.4 0.1 copy.29
  35.5 0.8 %all_to_all.17 = f32[64,1,512]{2,1,0:T(1,128)} reshape(f32[64,2,256]{2,1,0:T(2,128)S(1)} %copy.29) | data formatting | bytes 262144 | tf_op jit(solution)/shard_map/all_to_all | solution.py:100
  36.3 5.9 %all-to-all-start.1 = ((f32[64,1,512]{2,1,0:T(1,128)}), f32[64,1,512]{2,1,0:T(1,128)S(1)}, u32[]{:S(2)}, u32[]{:S(2)}) async-start(f32[64,1,512]{2,1,0:T(1,128)} %all_to_all.17), calls=%async_computation.1 | async-start | bytes 262144 | tf_op jit(solution)/shard_map/all_to_all | solution.py:100
  42.2 0.0 copy-done.6
  42.3 0.1 copy.22
  42.4 9.6 %all-to-all-done.1 = f32[64,1,512]{2,1,0:T(1,128)S(1)} async-done(((f32[64,1,512]{2,1,0:T(1,128)}), f32[64,1,512]{2,1,0:T(1,128)S(1)}, u32[]{:S(2)}, u32[]{:S(2)}) %all-to-all-start.1) | async-done | bytes 131104 | tf_op jit(solution)/shard_map/all_to_all | solution.py:100
  52.0 0.3 reduce.1
  52.3 0.0 copy-done.8
  52.4 0.1 multiply_reduce_fusion
  52.5 20.7 %psum.7 = f32[256]{0:T(256)S(1)} all-reduce(f32[256]{0:T(256)S(1)} %multiply_reduce_fusion), channel_id=1, replica_groups=mesh['seq'=64,'ch'=8] {'ch'}, use_global_device_ids=true, to_apply=%region_1.2 | all-reduce | flops 256 | bytes 2048 | tf_op jit(solution)/shard_map/psum | solution.py:103
  73.2 0.0 copy-done.9
  73.2 0.1 multiply_convert_fusion
  73.3 0.7 copy.32
  (6 shorter events, 0.1 us)
Async XLA Ops:
  0.0 30.2 %copy-start.1 = (bf16[528,256,1]{1,0,2:T(8,128)(2,1)S(1)}, bf16[528,256,1]{1,0,2:T(8,128)(2,1)}, u32[]{:S(2)}) copy-start(bf16[528,256,1]{1,0,2:T(8,128)(2,1)} %constant.40) | copy-start | bytes 811012
  0.0 30.6 %copy-start.7 = (f32[64,256,1]{1,0,2:T(8,128)S(1)}, f32[64,256,1]{1,0,2:T(8,128)}, u32[]{:S(2)}) copy-start(f32[64,256,1]{1,0,2:T(8,128)} %constant.41) | copy-start | bytes 196612
  32.1 0.9 %copy-start.2 = (f32[264,128]{1,0:T(8,128)S(1)}, f32[264,128]{1,0:T(8,128)}, u32[]{:S(2)}) copy-start(f32[264,128]{1,0:T(8,128)} %constant.38.clone) | copy-start | bytes 405508
  32.1 1.0 %copy-start.3 = (f32[264,128]{1,0:T(8,128)S(1)}, f32[264,128]{1,0:T(8,128)}, u32[]{:S(2)}) copy-start(f32[264,128]{1,0:T(8,128)} %constant.39.clone) | copy-start | bytes 405508
  32.3 1.1 %copy-start.5 = (f32[256,64,1]{0,1,2:T(8,128)S(1)}, f32[256,64,1]{0,1,2:T(8,128)}, u32[]{:S(2)}) copy-start(f32[256,64,1]{0,1,2:T(8,128)} %constant.42) | copy-start | bytes 196612
  32.3 1.8 %copy-start.4 = (f32[256,64,1]{0,1,2:T(8,128)S(1)}, f32[256,64,1]{0,1,2:T(8,128)}, u32[]{:S(2)}) copy-start(f32[256,64,1]{0,1,2:T(8,128)} %constant.43) | copy-start | bytes 196612
  32.3 2.5 %copy-start = (f32[256,528,1]{0,1,2:T(8,128)S(1)}, f32[256,528,1]{0,1,2:T(8,128)}, u32[]{:S(2)}) copy-start(f32[256,528,1]{0,1,2:T(8,128)} %constant.44) | copy-start | bytes 1622020
  33.0 9.2 %copy-start.6 = (bf16[256,128]{1,0:T(8,128)(2,1)S(1)}, bf16[256,128]{1,0:T(8,128)(2,1)}, u32[]{:S(2)}) copy-start(bf16[256,128]{1,0:T(8,128)(2,1)} %param.14) | copy-start | bytes 196612
  33.2 19.1 %copy-start.8 = (f32[128]{0:T(128)S(1)}, f32[128]{0:T(128)}, u32[]{:S(2)}) copy-start(f32[128]{0:T(128)} %param.17) | copy-start | bytes 1540
  33.2 39.9 %copy-start.9 = (f32[128]{0:T(128)S(1)}, f32[128]{0:T(128)}, u32[]{:S(2)}) copy-start(f32[128]{0:T(128)} %param.18) | copy-start | bytes 1540
  36.3 15.7 %all-to-all-start.1 = ((f32[64,1,512]{2,1,0:T(1,128)}), f32[64,1,512]{2,1,0:T(1,128)S(1)}, u32[]{:S(2)}, u32[]{:S(2)}) async-start(f32[64,1,512]{2,1,0:T(1,128)} %all_to_all.17), calls=%async_computation.1 | async-start | bytes 262144 | tf_op jit(solution)/shard_map/all_to_all | solution.py:100
where the time goes:
time: 74.3 us; the launch traced here: 74 us
  blocking collectives  43.4 us (58%)
  waiting for transfers between devices  9.63 us (13%)
  starting transfers between devices  5.94 us (8%)
  local copies, waits for them, and re-layouts  5.73 us (8%)
  other arithmetic  5.16 us (7%)
  matrix products  3.82 us (5%)
    all_to_all x1, blocking collectives, on_device(): recv = lax.all_to_all(send, 'seq', 0, 0, tiled=True)  22.8 us
    psum x1, blocking collectives, on_device(): squares = lax.psum(jnp.sum(gated_mix * gated_mix, axis=1), 'ch')  20.7 us
    all_to_all x1, waiting for transfers between devices, on_device(): got = lax.all_to_all(back, 'seq', 0, 0, tiled=True)  9.63 us
    all_to_all x1, starting transfers between devices, on_device(): got = lax.all_to_all(back, 'seq', 0, 0, tiled=True)  5.94 us
    unnamed x25, local copies, waits for them, and re-layouts  3.02 us
    all_to_all x2, other arithmetic, on_device(): recv = lax.all_to_all(send, 'seq', 0, 0, tiled=True)  2.93 us
    dot_general x1, matrix products, on_device(): jnp.einsum('qfb,bk->qfk', spec, ofwd, precision=HIGHEST, preferred_elemen...  1.49 us
  transfers between devices with their start and end apart: 1, of which 1 were waited for; matrix products, arithmetic and copies ran while one was open for 0% of the time, Pallas kernels for 0%

commit v1 on v0

--- a/solution.py
+++ b/solution.py
@@ -100,7 +100,9 @@
     got = lax.all_to_all(back, "seq", 0, 0, tiled=True)
     convolved = got.reshape(blocks * per, rows_dev).T
     gated_mix = gate_values.astype(f32) * (convolved + skip_gain[None, :] * inputs.astype(f32))
-    squares = lax.psum(jnp.sum(gated_mix * gated_mix, axis=1), "ch")
+    block = jnp.sum(gated_mix * gated_mix, axis=1)
+    parts = lax.all_gather(block, "ch")
+    squares = jnp.sum(parts, axis=0)
     inv_norm = lax.rsqrt(squares / D + 1e-06)
     return (norm_gain[None, :] * gated_mix * inv_norm[:, None]).astype(jnp.bfloat16)
 

time: 74.3 us -> 73 us (0.983)
  blocking collectives: 43.4 us -> 42.1 us
    psum x1 -> x0, blocking collectives: 20.7 us -> none  [on_device(): squares = lax.psum(jnp.sum(gated_mix * gated_mix, axis=1), 'ch')]
    all_gather x0 -> x1, blocking collectives: none -> 19.3 us  [on_device(): parts = lax.all_gather(block, 'ch')]
where the time goes in v1:
time: 73 us; the launch traced here: 72.7 us
  blocking collectives  42.1 us (58%)
  waiting for transfers between devices  9.63 us (13%)
  starting transfers between devices  5.94 us (8%)
  local copies, waits for them, and re-layouts  5.73 us (8%)
  other arithmetic  5.19 us (7%)
  matrix products  3.82 us (5%)
    all_to_all x1, blocking collectives, on_device(): recv = lax.all_to_all(send, 'seq', 0, 0, tiled=True)  22.8 us
    all_gather x1, blocking collectives, on_device(): parts = lax.all_gather(block, 'ch')  19.3 us
    all_to_all x1, waiting for transfers between devices, on_device(): got = lax.all_to_all(back, 'seq', 0, 0, tiled=True)  9.63 us
    all_to_all x1, starting transfers between devices, on_device(): got = lax.all_to_all(back, 'seq', 0, 0, tiled=True)  5.94 us
    unnamed x25, local copies, waits for them, and re-layouts  3.02 us
    all_to_all x2, other arithmetic, on_device(): recv = lax.all_to_all(send, 'seq', 0, 0, tiled=True)  2.93 us
    dot_general x1, matrix products, on_device(): jnp.einsum('qfb,bk->qfk', spec, ofwd, precision=HIGHEST, preferred_elemen...  1.49 us
  transfers between devices with their start and end apart: 1, of which 1 were waited for; matrix products, arithmetic and copies ran while one was open for 0% of the time, Pallas kernels for 0%

profile of v1, /device:TPU:1, one launch (start us, length us, event | category | flops | bytes accessed | tf_op | source)
XLA Modules:
  0.0 72.7 jit_solution(17783272990708882191)
XLA Ops:
  0.0 0.0 copy-start.1
  0.0 0.0 copy-start.7
  0.0 1.0 %copy.23 = bf16[256,128]{0,1:T(8,128)(2,1)S(1)} copy(bf16[256,128]{1,0:T(8,128)(2,1)} %param.13) | data formatting | bytes 131072 | tf_op args[0]
  1.1 0.9 %broadcast_select_fusion = bf16[256,128]{1,0:T(8,128)(2,1)S(1)} fusion(bf16[256,128]{1,0:T(8,128)(2,1)} %param.16, pred[256]{0:T(512)(128)(4,1)S(1)} %add_compare_fusion), kind=kLoop, calls=%fused_computation.22 | loop fusion | flops 32768 | bytes 131328 | tf_op jit(solution)/shard_map/jit(_where)/select_n | solution.py:62
  2.0 0.1 copy.25
  2.2 0.9 %copy.24 = bf16[256,128]{0,1:T(8,128)(2,1)S(1)} copy(bf16[256,128]{1,0:T(8,128)(2,1)} %param.15) | data formatting | bytes 131072 | tf_op args[2]
  3.1 0.3 maximum_bitcast_fusion
  3.5 0.1 copy.26
  3.6 0.1 all_to_all.16
  3.8 0.5 broadcast.25
  4.3 1.8 %reduce.3 = bf16[64,1536]{1,0:T(8,128)(2,1)S(1)} reduce(bf16[64,1,1536]{2,1,0:T(2,128)(2,1)S(1)} %all_to_all.16, bf16[]{:T(256)} %broadcast.25), dimensions={1}, to_apply=%all_to_all.16.reduce_sub_computation | reduce | bytes 393218 | tf_op jit(solution)/shard_map/all_to_all | solution.py:78
  6.1 0.1 reshape.66
  6.1 22.8 %all_to_all.20 = bf16[64,2,768]{2,1,0:T(2,128)(2,1)S(1)} all-to-all(bf16[64,2,768]{2,1,0:T(2,128)(2,1)S(1)} %reshape.66), channel_id=1, replica_groups=mesh['seq'=64,'ch'=8] {'seq'}, dimensions={0} | all-to-all | bytes 393216 | tf_op jit(solution)/shard_map/all_to_all | solution.py:78
  28.9 0.1 reshape.67
  29.0 1.1 %reduce.1 = bf16[64,1536]{1,0:T(8,128)(2,1)S(1)} reduce(bf16[64,1,1536]{2,1,0:T(2,128)(2,1)S(1)} %reshape.67, bf16[]{:T(256)} %constant.45), dimensions={1}, to_apply=%all_to_all.13.reduce_sub_computation | reduce | bytes 393218 | tf_op jit(solution)/shard_map/all_to_all | solution.py:78
  30.2 0.0 copy-done.1
  30.2 0.3 fusion
  30.6 0.0 copy-done.7
  30.6 1.5 %fusion.11 = f32[6,528,256]{2,1,0:T(8,128)S(1)} fusion(bf16[6,528,64]{1,2,0:T(8,128)(2,1)S(1)} %fusion, f32[64,256,1]{1,0,2:T(8,128)S(1)} %copy-done.7), kind=kOutput, calls=%fused_computation.28 | convolution fusion | flops 622854144 | bytes 3715072 | tf_op jit(solution)/shard_map/qfb,bk->qfk/dot_general | solution.py:82
  32.1 0.0 copy-start.2
  32.1 0.0 copy-start.3
  32.1 0.2 slice_add_fusion
  32.3 0.0 copy-start.5
  32.3 0.0 copy-start.4
  32.3 0.0 copy-start
  32.3 0.7 copy-done.2
  33.0 0.1 copy-done.3
  33.0 0.0 copy-start.6
  33.0 0.2 multiply_subtract_fusion
  33.2 0.0 copy-start.8
  33.2 0.0 copy-start.9
  33.3 0.1 multiply_add_fusion
  33.3 0.0 copy-done.5
  33.3 0.7 %fusion.2 = f32[2,264,64]{1,2,0:T(8,128)S(1)} fusion(f32[256,64,1]{0,1,2:T(8,128)S(1)} %copy-done.5, f32[2,264,128]{2,1,0:T(8,128)S(1)} %multiply_add_fusion, f32[2,264,128]{2,1,0:T(8,128)S(1)} %get-tuple-element.5), kind=kOutput, calls=%fused_computation.7 | convolution fusion | flops 103944192 | bytes 741376 | tf_op jit(solution)/shard_map/cfk,ki->cfi/dot_general | solution.py:95
  34.1 0.0 copy-done.4
  34.1 0.7 %fusion.1 = f32[2,264,64]{1,2,0:T(8,128)S(1)} fusion(f32[256,64,1]{0,1,2:T(8,128)S(1)} %copy-done.4, f32[2,264,128]{2,1,0:T(8,128)S(1)} %multiply_add_fusion, f32[2,264,128]{2,1,0:T(8,128)S(1)} %get-tuple-element.5), kind=kOutput, calls=%fused_computation.6 | convolution fusion | flops 103944192 | bytes 741376 | tf_op jit(solution)/shard_map/cfk,ki->cfi/dot_general | solution.py:96
  34.8 0.0 copy-done
  34.8 0.5 convolution_bitcast_fusion
  35.4 0.1 copy.29
  35.5 0.8 %all_to_all.17 = f32[64,1,512]{2,1,0:T(1,128)} reshape(f32[64,2,256]{2,1,0:T(2,128)S(1)} %copy.29) | data formatting | bytes 262144 | tf_op jit(solution)/shard_map/all_to_all | solution.py:100
  36.3 5.9 %all-to-all-start.1 = ((f32[64,1,512]{2,1,0:T(1,128)}), f32[64,1,512]{2,1,0:T(1,128)S(1)}, u32[]{:S(2)}, u32[]{:S(2)}) async-start(f32[64,1,512]{2,1,0:T(1,128)} %all_to_all.17), calls=%async_computation.1 | async-start | bytes 262144 | tf_op jit(solution)/shard_map/all_to_all | solution.py:100
  42.2 0.0 copy-done.6
  42.3 0.1 copy.22
  42.4 9.6 %all-to-all-done.1 = f32[64,1,512]{2,1,0:T(1,128)S(1)} async-done(((f32[64,1,512]{2,1,0:T(1,128)}), f32[64,1,512]{2,1,0:T(1,128)S(1)}, u32[]{:S(2)}, u32[]{:S(2)}) %all-to-all-start.1) | async-done | bytes 131104 | tf_op jit(solution)/shard_map/all_to_all | solution.py:100
  52.0 0.3 reduce.2
  52.3 0.0 copy-done.8
  52.4 0.1 multiply_reduce_fusion
  52.5 19.3 %all-gather.1 = f32[8,1,256]{2,1,0:T(1,128)S(1)} all-gather(f32[1,1,256]{2,1,0:T(1,128)S(1)} %bitcast.40), channel_id=2, replica_groups=mesh['seq'=64,'ch'=8] {'ch'}, dimensions={0}, use_global_device_ids=true | all-gather | bytes 9216 | tf_op jit(solution)/shard_map/all_gather | solution.py:104
  71.8 0.0 copy-done.9
  71.8 0.1 multiply_convert_fusion
  72.0 0.7 %copy.32 = bf16[256,128]{1,0:T(8,128)(2,1)} copy(bf16[256,128]{0,1:T(8,128)(2,1)S(1)} %multiply_convert_fusion) | data formatting | bytes 131072 | tf_op jit(solution)/shard_map/convert_element_type | solution.py:107
  (7 shorter events, 0.2 us)
Async XLA Ops:
  0.0 30.2 %copy-start.1 = (bf16[528,256,1]{1,0,2:T(8,128)(2,1)S(1)}, bf16[528,256,1]{1,0,2:T(8,128)(2,1)}, u32[]{:S(2)}) copy-start(bf16[528,256,1]{1,0,2:T(8,128)(2,1)} %constant.40) | copy-start | bytes 811012
  0.0 30.6 %copy-start.7 = (f32[64,256,1]{1,0,2:T(8,128)S(1)}, f32[64,256,1]{1,0,2:T(8,128)}, u32[]{:S(2)}) copy-start(f32[64,256,1]{1,0,2:T(8,128)} %constant.41) | copy-start | bytes 196612
  32.1 0.9 %copy-start.2 = (f32[264,128]{1,0:T(8,128)S(1)}, f32[264,128]{1,0:T(8,128)}, u32[]{:S(2)}) copy-start(f32[264,128]{1,0:T(8,128)} %constant.38.clone) | copy-start | bytes 405508
  32.1 1.0 %copy-start.3 = (f32[264,128]{1,0:T(8,128)S(1)}, f32[264,128]{1,0:T(8,128)}, u32[]{:S(2)}) copy-start(f32[264,128]{1,0:T(8,128)} %constant.39.clone) | copy-start | bytes 405508
  32.3 1.1 %copy-start.5 = (f32[256,64,1]{0,1,2:T(8,128)S(1)}, f32[256,64,1]{0,1,2:T(8,128)}, u32[]{:S(2)}) copy-start(f32[256,64,1]{0,1,2:T(8,128)} %constant.42) | copy-start | bytes 196612
  32.3 1.8 %copy-start.4 = (f32[256,64,1]{0,1,2:T(8,128)S(1)}, f32[256,64,1]{0,1,2:T(8,128)}, u32[]{:S(2)}) copy-start(f32[256,64,1]{0,1,2:T(8,128)} %constant.43) | copy-start | bytes 196612
  32.3 2.5 %copy-start = (f32[256,528,1]{0,1,2:T(8,128)S(1)}, f32[256,528,1]{0,1,2:T(8,128)}, u32[]{:S(2)}) copy-start(f32[256,528,1]{0,1,2:T(8,128)} %constant.44) | copy-start | bytes 1622020
  33.0 9.2 %copy-start.6 = (bf16[256,128]{1,0:T(8,128)(2,1)S(1)}, bf16[256,128]{1,0:T(8,128)(2,1)}, u32[]{:S(2)}) copy-start(bf16[256,128]{1,0:T(8,128)(2,1)} %param.14) | copy-start | bytes 196612
  33.2 19.1 %copy-start.8 = (f32[128]{0:T(128)S(1)}, f32[128]{0:T(128)}, u32[]{:S(2)}) copy-start(f32[128]{0:T(128)} %param.17) | copy-start | bytes 1540
  33.2 38.6 %copy-start.9 = (f32[128]{0:T(128)S(1)}, f32[128]{0:T(128)}, u32[]{:S(2)}) copy-start(f32[128]{0:T(128)} %param.18) | copy-start | bytes 1540
  36.3 15.7 %all-to-all-start.1 = ((f32[64,1,512]{2,1,0:T(1,128)}), f32[64,1,512]{2,1,0:T(1,128)S(1)}, u32[]{:S(2)}, u32[]{:S(2)}) async-start(f32[64,1,512]{2,1,0:T(1,128)} %all_to_all.17), calls=%async_computation.1 | async-start | bytes 262144 | tf_op jit(solution)/shard_map/all_to_all | solution.py:100
